TPU v7x, 32 devices: a whole 2x2x4 slice. The times are simulated.
32 devices in a mesh: seq: 8 (over z, y), mp: 4 (over x, core).
Axes of the slice: x: 2, y: 2, z: 4, core: 2. Of those that a mesh axis runs over, the one named last changes fastest.
Arguments:
- query: bfloat16 [3840, 5120], P('seq', 'mp'), may hold values from -32 to 32
- query_gain: float32 [5120], P('mp'), may hold values from 0.25 to 1.75
- cond: bfloat16 [8, 2, 128, 5120], P('seq', None, None, 'mp'), may hold values from -32 to 32
- key_gain: float32 [5120], P('mp'), may hold values from 0.25 to 1.75
- grad_out: bfloat16 [3840, 5120], P('seq', 'mp'), may hold values from -15 to 15
- clip_len: int32 [3], replicated, may hold values from 1 to 1920, 3840 in all
- clip_owner: int32 [3], replicated, may hold values from 0 to 7, as said below
Outputs:
- grad_query: bfloat16 [3840, 5120], P('seq', 'mp')
- grad_cond: bfloat16 [8, 2, 128, 5120], P('seq', None, None, 'mp')
Inputs may be any that keep to these rules, and one draw needn't show every extreme that they name: `clip_len`: the clip lengths sum to 3840, and the longest is exactly 1920. `clip_owner`: the owners of the 3 clips are distinct slots.
All inputs are finite; a program needn't handle non-finite values.
Results may differ from a plain program's by a relative error of at most 0.011.
Values may be sent and summed in bfloat16 or wider, within the bound.
No kernel may reach another device: no remote copies, remote signals or barrier semaphores. Data moves between devices by JAX's collectives and lax.ppermute only.
A program may use at most 128 MiB of HBM per device.

v0:
```python
import math
import jax
import jax.numpy as jnp
from jax import lax
from jax.sharding import PartitionSpec as P

D = 5120
HEAD_DIM = 128
EPS = 1e-06
MASKED = -1e30


def broadcast(value, axis, root):
    mine = lax.axis_index(axis) == root
    return lax.psum(jnp.where(mine, value, jnp.zeros_like(value)), axis)


def attend(query_heads, key_heads, value_heads, grad_heads, allowed, score_scale):
    scores = (
        jnp.einsum("thd,khd->htk", query_heads, key_heads, preferred_element_type=jnp.float32)
        * score_scale
    )
    scores = jnp.where(allowed[None, :, :], scores, MASKED)
    row_max = jnp.max(scores, axis=2, keepdims=True)
    weights = jnp.exp(scores - row_max)
    normed_weights = weights / jnp.sum(weights, axis=2, keepdims=True)
    weights_low = normed_weights.astype(jnp.bfloat16)
    attended = jnp.einsum(
        "htk,khd->thd", weights_low, value_heads, preferred_element_type=jnp.float32
    ).astype(jnp.bfloat16)
    delta = jnp.sum(grad_heads.astype(jnp.float32) * attended.astype(jnp.float32), axis=2)
    grad_weights = jnp.einsum(
        "thd,khd->htk", grad_heads, value_heads, preferred_element_type=jnp.float32
    )
    grad_scores = (
        normed_weights * (grad_weights - jnp.transpose(delta)[:, :, None]) * score_scale
    ).astype(jnp.bfloat16)
    grad_q = jnp.einsum("htk,khd->thd", grad_scores, key_heads, preferred_element_type=jnp.float32)
    grad_k = jnp.einsum(
        "htk,thd->khd", grad_scores, query_heads, preferred_element_type=jnp.float32
    )
    grad_v = jnp.einsum("htk,thd->khd", weights_low, grad_heads, preferred_element_type=jnp.float32)
    return (grad_q, grad_k, grad_v)


def local(query, query_gain, cond, key_gain, grad_out, clip_len, clip_owner):
    tok_rows = query.shape[0]
    feat_width = query.shape[1]
    head_count = feat_width // HEAD_DIM
    clip_count = clip_len.shape[0]
    cond_depth = cond.shape[2]
    my_index = lax.axis_index("seq")
    first_pos = my_index * tok_rows
    position = first_pos + jnp.arange(tok_rows, dtype=jnp.int32)
    starts = jnp.cumsum(clip_len) - clip_len
    clip_of = jnp.sum((position[:, None] >= starts[None, :]).astype(jnp.int32), axis=1) - 1
    query_wide = query.astype(jnp.float32)
    query_sumsq = lax.psum(jnp.sum(query_wide * query_wide, axis=1), "mp")
    query_scale = lax.rsqrt(query_sumsq / D + EPS)
    query_normed = (query_wide * query_scale[:, None] * query_gain).astype(jnp.bfloat16)
    slab_stack = jnp.stack(
        [broadcast(cond[0], "seq", clip_owner[clip_index]) for clip_index in range(clip_count)]
    )
    key_raw = slab_stack[:, 0].astype(jnp.float32)
    key_sumsq = lax.psum(jnp.sum(key_raw * key_raw, axis=2), "mp")
    key_scale = lax.rsqrt(key_sumsq / D + EPS)
    key_normed = (key_raw * key_scale[:, :, None] * key_gain).astype(jnp.bfloat16)
    key_heads = key_normed.reshape(clip_count, cond_depth, head_count, HEAD_DIM)
    value_heads = slab_stack[:, 1].reshape(clip_count, cond_depth, head_count, HEAD_DIM)
    query_heads = query_normed.reshape(tok_rows, head_count, HEAD_DIM)
    grad_heads = grad_out.reshape(tok_rows, head_count, HEAD_DIM)
    score_scale = 1.0 / math.sqrt(HEAD_DIM)
    key_clip = jnp.arange(clip_count * cond_depth, dtype=jnp.int32) // cond_depth
    allowed = clip_of[:, None] == key_clip[None, :]
    grad_query_wide, grad_keys_flat, grad_values_flat = attend(
        query_heads,
        key_heads.reshape(clip_count * cond_depth, head_count, HEAD_DIM),
        value_heads.reshape(clip_count * cond_depth, head_count, HEAD_DIM),
        grad_heads,
        allowed,
        score_scale,
    )
    key_grad = grad_keys_flat.reshape(clip_count, cond_depth, feat_width)
    value_grad = grad_values_flat.reshape(clip_count, cond_depth, feat_width)
    grad_query = grad_query_wide.reshape(tok_rows, feat_width).astype(jnp.bfloat16)
    partial_grads = jnp.stack([key_grad, value_grad], axis=1)
    owner_mask = (clip_owner == my_index).astype(jnp.float32)
    summed = lax.psum(partial_grads, "seq")
    owned_grads = jnp.sum(summed * owner_mask[:, None, None, None], axis=0).astype(jnp.bfloat16)
    return (grad_query, owned_grads[None])


def solution(mesh):
    return jax.shard_map(
        local,
        mesh=mesh,
        in_specs=(
            P("seq", "mp"),
            P("mp"),
            P("seq", None, None, "mp"),
            P("mp"),
            P("seq", "mp"),
            P(),
            P(),
        ),
        out_specs=(P("seq", "mp"), P("seq", None, None, "mp")),
        check_vma=False,
    )
```

profile of v0, /device:TPU:0, one launch (start us, length us, event | category | flops | bytes accessed | tf_op | source)
XLA Modules:
  0.0 390.9 jit_solution(13383794463649991475)
XLA Ops:
  7.2 0.0 all-reduce.7.cloned.1.call-start
  7.2 1.4 fusion.21
  10.6 2.4 broadcast_select_fusion
  13.1 0.0 all-reduce.7.cloned.1.call-update
  13.1 0.0 all-reduce.5.cloned.1.call-start
  13.1 0.0 copy-start.11
  13.1 0.0 copy-start.5
  13.2 1.7 copy.50
  14.8 1.5 copy.53
  16.3 0.0 copy-done.11
  16.3 0.2 reduce-window.9
  16.5 0.1 convert_reduce_fusion
  16.6 0.0 copy-done.5
  16.6 0.3 fusion.8
  16.9 0.2 broadcast_compare_fusion
  17.1 98.0 %all-reduce.7.cloned.1.call-done = (bf16[1,2,128,1280]{3,2,1,0:T(8,128)(2,1)}, bf16[1,2,128,1280]{3,2,1,0:T(8,128)(2,1)}, bf16[1,2,128,1280]{3,2,1,0:T(8,128)(2,1)}) async-done(((bf16[1,2,128,1280]{3,2,1,0:T(8,128)(2,1)}, bf16[1,2,128,1280]{3,2,1,0:T(8,128)(2,1)}, bf16[1,2,128,1280]{3,2,1,0:T(8,128)(2,1)}), (bf16[1,2,128,1280]{3,2,1,0:T(8,128)(2,1)}, bf16[1,2,128,1280]{3,2,1,0:T(8,128)(2,1)}, ...) | async-done | bytes 1966096 | tf_op jit(solution)/shard_map/psum | solution.py:15
  115.1 0.0 copy-start.7
  115.1 1.2 constant_dynamic-update-slice_fusion.2
  116.3 1.1 constant_dynamic-update-slice_fusion.1
  117.4 0.0 copy-done.7
  117.5 0.3 multiply_reduce_fusion.1
  117.7 1.2 fusion.20
  118.9 6.8 %all-reduce = (f32[3,128]{1,0:T(4,128)S(1)}, f32[480]{0:T(512)S(1)}) all-reduce(f32[3,128]{1,0:T(4,128)S(1)} %multiply_reduce_fusion.1, f32[480]{0:T(512)S(1)} %fusion.8), channel_id=1, replica_groups=mesh['seq'=8,'mp'=4] {'mp'}, use_global_device_ids=true, to_apply=%region_4.5 | all-reduce | flops 864 | bytes 6912 | tf_op jit(solution)/shard_map/psum | solution.py:65
  125.7 0.0 copy-start.8
  125.7 3.4 copy.49
  129.1 3.7 reshape_reshape_squeeze.3
  132.8 0.0 copy-done.8
  132.8 2.7 fusion.10
  135.5 2.4 copy.46
  137.9 2.6 copy.45
  140.6 0.0 copy-start.9
  140.6 3.1 reshape.127
  143.6 0.0 copy-start.2
  143.7 0.0 copy-done.9
  143.7 7.8 %fusion.22 = (f32[10,480]{1,0:T(8,128)S(1)}, f32[10,480,384]{2,1,0:T(8,128)}) fusion(pred[480,384]{1,0:T(8,128)(4,1)S(1)} %broadcast_compare_fusion, bf16[480,10,128]{0,2,1:T(8,128)(2,1)} %bitcast.55, f32[384,10,128]{0,2,1:T(8,128)S(1)} %reshape.127, f32[10,128]{1,0:T(8,128)S(1)} %bitcast.58, f32[384]{0:T(512)S(1)} %rsqrt_bitcast_fusion), kind=kOutput, calls=%fused_computation.56 | convolution fusion | flops 480706944 | bytes 10777856 | tf_op jit(solution)/shard_map/sub | solution.py:25
  151.5 0.0 copy-done.2
  151.5 3.6 fusion.7
  155.1 0.0 copy-start.1
  155.1 1.9 copy-done.1
  157.0 1.4 convolution_bitcast_fusion
  158.4 1.8 copy.59
  160.2 0.0 copy-start.6
  160.2 4.0 %fusion.11 = f32[480,10]{0,1:T(8,128)S(1)} fusion(bf16[480,10,128]{2,0,1:T(8,128)(2,1)} %copy.53, bf16[384,10,128]{0,2,1:T(8,128)(2,1)} %reshape_reshape_squeeze.3, bf16[10,480,384]{2,1,0:T(8,128)(2,1)} %copy-done.1), kind=kOutput, calls=%fused_computation.20 | convolution fusion | flops 474926400 | bytes 5917440 | tf_op jit(solution)/shard_map/htk,khd->thd/dot_general | solution.py:28
  164.2 0.0 copy-done.6
  164.2 0.0 copy-start.4
  164.2 4.4 %fusion.2 = bf16[10,480,384]{2,1,0:T(8,128)(2,1)S(1)} fusion(f32[10,480]{1,0:T(8,128)S(1)} %bitcast.61, f32[10,480,384]{2,1,0:T(8,128)} %get-tuple-element.22, f32[10,480]{1,0:T(8,128)S(1)} %get-tuple-element.21, bf16[384,10,128]{0,2,1:T(8,128)(2,1)S(1)} %copy-done.6, bf16[480,10,128]{0,2,1:T(8,128)(2,1)S(1)} %bitcast.53), kind=kOutput, calls=%fused_computation.3 | convolution fusion | flops 481075200 | bytes 13309440 | tf_op jit(solution)/shard_map/thd,khd->htk/dot_general | solution.py:32
  168.6 0.0 copy-start
  168.6 1.9 copy-done
  170.5 0.0 copy-done.4
  170.5 2.1 convolution_bitcast_fusion.1
  172.7 2.7 stack_reshape.6
  175.4 4.0 %stack_reshape.7 = f32[3,1,128,1280]{2,0,3,1:T(4,128)} reshape(f32[384,10,128]{0,2,1:T(8,128)} %copy.59) | data formatting | bytes 3932160 | tf_op jit(solution)/shard_map/stack;reshape | solution.py:86
  179.4 5.0 %pad_maximum_fusion = f32[3,2,128,1280]{2,0,3,1:T(4,128)} fusion(f32[3,1,128,1280]{2,0,3,1:T(4,128)} %stack_reshape.7, f32[3,1,128,1280]{2,0,3,1:T(4,128)S(1)} %stack_reshape.6), kind=kLoop, calls=%fused_computation.7 | loop fusion | flops 983040 | bytes 7864320 | tf_op jit(solution)/shard_map/stack | solution.py:86
  184.5 0.0 copy-start.10
  184.5 0.0 copy-start.3
  184.5 0.0 all-reduce.5.cloned.1.call-update
  184.5 0.6 copy-done.10
  185.1 0.9 copy-done.3
  186.0 3.2 fusion.12
  189.3 0.6 copy.56
  189.9 1.5 copy.60
  191.4 176.1 %all-reduce.5.cloned.1.call-done = f32[3,2,128,1280]{2,0,3,1:T(4,128)} async-done(((f32[3,2,128,1280]{2,0,3,1:T(4,128)}), f32[3,2,128,1280]{2,0,3,1:T(4,128)}) %all-reduce.5.cloned.1.call-update) | async-done | bytes 3932176 | tf_op jit(solution)/shard_map/psum | solution.py:88
  367.5 15.5 %multiply_reduce_fusion = bf16[2,128,1280]{1,2,0:T(8,128)(2,1)S(1)} fusion(f32[3,2,128,1280]{2,0,3,1:T(4,128)} %all-reduce.5.cloned.1.call-done, f32[3]{0:T(128)S(1)} %compare_convert_fusion), kind=kLoop, calls=%fused_computation.8 | loop fusion | flops 1638400 | bytes 4587532 | tf_op jit(solution)/shard_map/reduce_sum | solution.py:89
  383.0 1.1 copy.61
  (8 shorter events, 0.1 us)
Async XLA Ops:
  7.2 107.9 %all-reduce.7.cloned.1.call-start = ((), (), s32[]{:S(2)}) async-start(), calls=%async_computation.1 | async-start | bytes 3932160 | tf_op jit(solution)/shard_map/psum | solution.py:15
  13.1 354.4 %all-reduce.5.cloned.1.call-start = ((), (), s32[]{:S(2)}) async-start(), calls=%async_computation | async-start | bytes 10485760 | tf_op jit(solution)/shard_map/psum | solution.py:88
  13.1 3.2 copy-start.11
  13.1 3.5 copy-start.5
  115.1 2.3 copy-start.7
  125.7 7.1 %copy-start.8 = (f32[1280]{0:T(1024)S(1)}, f32[1280]{0:T(1024)}, u32[]{:S(2)}) copy-start(f32[1280]{0:T(1024)} %param.8) | copy-start | bytes 15364
  140.6 3.1 copy-start.9
  143.6 7.9 %copy-start.2 = (f32[384,10,128]{0,2,1:T(8,128)}, f32[384,10,128]{0,2,1:T(8,128)S(1)}, u32[]{:S(2)}) copy-start(f32[384,10,128]{0,2,1:T(8,128)S(1)} %reshape.127) | copy-start | bytes 5898244
  155.1 1.9 copy-start.1
  160.2 4.0 %copy-start.6 = (bf16[384,10,128]{0,2,1:T(8,128)(2,1)S(1)}, bf16[384,10,128]{0,2,1:T(8,128)(2,1)}, u32[]{:S(2)}) copy-start(bf16[384,10,128]{0,2,1:T(8,128)(2,1)} %reshape_reshape_squeeze.3) | copy-start | bytes 2949124
  164.2 6.3 %copy-start.4 = (bf16[480,1280]{0,1:T(8,128)(2,1)S(1)}, bf16[480,1280]{0,1:T(8,128)(2,1)}, u32[]{:S(2)}) copy-start(bf16[480,1280]{0,1:T(8,128)(2,1)} %copy.46) | copy-start | bytes 3686404
  168.6 1.9 copy-start
  184.5 0.7 copy-start.10
  184.5 1.6 copy-start.3
Sparse Core Ops, SparseCore 0:
  13.2 101.8 all-reduce.6
  184.6 182.7 all-reduce.4
where the time goes:
time: 392 us; the launch traced here: 391 us
  waiting for transfers between devices  274 us (70%)
  local copies, waits for them, and re-layouts  39.3 us (10%)
  other arithmetic  31.4 us (8%)
  matrix products  23 us (6%)
  between operations  16.2 us (4%)
  blocking collectives  6.81 us (2%)
    psum x1, waiting for transfers between devices, local(): summed = lax.psum(partial_grads, 'seq')  176 us
    psum x1, waiting for transfers between devices, broadcast(): return lax.psum(jnp.where(mine, value, jnp.zeros_like(value)), axis)  98 us
    reduce_sum x1, other arithmetic, local(): jnp.sum(summed * owner_mask[:, None, None, None], axis=0)  15.5 us
    unnamed x29, local copies, waits for them, and re-layouts  12 us
    sub x1, matrix products, attend(): weights = jnp.exp(scores - row_max)  7.85 us
  transfers between devices with their start and end apart: 2, of which 2 were waited for; matrix products, arithmetic and copies ran while one was open for 2% of the time, Pallas kernels for 0%

commit v1 on v0

--- a/solution.py
+++ b/solution.py
@@ -85,7 +85,7 @@
     grad_query = grad_query_wide.reshape(tok_rows, feat_width).astype(jnp.bfloat16)
     partial_grads = jnp.stack([key_grad, value_grad], axis=1)
     owner_mask = (clip_owner == my_index).astype(jnp.float32)
-    summed = lax.psum(partial_grads, "seq")
+    summed = lax.all_gather(partial_grads, "seq").sum(axis=0)
     owned_grads = jnp.sum(summed * owner_mask[:, None, None, None], axis=0).astype(jnp.bfloat16)
     return (grad_query, owned_grads[None])
 

time: 392 us -> 813 us (2.07)
  waiting for transfers between devices: 274 us -> 688 us
    all_gather x0 -> x1, waiting for transfers between devices: none -> 590 us  [local(): summed = lax.all_gather(partial_grads, 'seq').sum(axis=0)]
    psum x1 -> x0, waiting for transfers between devices: 176 us -> none  [local(): summed = lax.psum(partial_grads, 'seq')]
    reduce_sum x0 -> x1, other arithmetic: none -> 13.4 us  [local(): summed = lax.all_gather(partial_grads, 'seq').sum(axis=0)]
    reduce_sum x1, other arithmetic: 15.5 us -> 3.52 us  [local(): jnp.sum(summed * owner_mask[:, None, None, None], axis=0)]
  transfers between devices with their start and end apart: 2 -> 2, of which waited for: 2 -> 2; matrix products, arithmetic and copies ran while one was open for 2% -> 1% of each run, Pallas kernels for 0% -> 0%
where the time goes in v1:
time: 813 us; the launch traced here: 812 us
  waiting for transfers between devices  688 us (85%)
  local copies, waits for them, and re-layouts  44.8 us (6%)
  other arithmetic  32.9 us (4%)
  matrix products  23 us (3%)
  between operations  16.2 us (2%)
    all_gather x1, waiting for transfers between devices, local(): summed = lax.all_gather(partial_grads, 'seq').sum(axis=0)  590 us
    psum x1, waiting for transfers between devices, broadcast(): return lax.psum(jnp.where(mine, value, jnp.zeros_like(value)), axis)  98 us
  transfers between devices with their start and end apart: 2, of which 2 were waited for; matrix products, arithmetic and copies ran while one was open for 1% of the time, Pallas kernels for 0%

profile of v1, /device:TPU:0, one launch (start us, length us, event | category | flops | bytes accessed | tf_op | source)
XLA Modules:
  0.0 812.4 jit_solution(1122063285126369907)
XLA Ops:
  7.2 0.0 all-reduce.4.cloned.1.call-start
  7.2 1.4 fusion.21
  10.6 2.4 broadcast_select_fusion
  13.1 0.0 all-reduce.4.cloned.1.call-update
  13.1 0.0 all-gather.3.cloned.1.call-start
  13.1 0.0 copy-start.11
  13.1 0.0 copy-start.5
  13.2 1.7 copy.51
  14.8 1.5 copy.54
  16.3 0.0 copy-done.11
  16.3 0.2 reduce-window.9
  16.5 0.1 convert_reduce_fusion
  16.6 0.0 copy-done.5
  16.6 0.3 fusion.8
  16.9 0.2 broadcast_compare_fusion
  17.1 98.0 %all-reduce.4.cloned.1.call-done = (bf16[1,2,128,1280]{3,2,1,0:T(8,128)(2,1)}, bf16[1,2,128,1280]{3,2,1,0:T(8,128)(2,1)}, bf16[1,2,128,1280]{3,2,1,0:T(8,128)(2,1)}) async-done(((bf16[1,2,128,1280]{3,2,1,0:T(8,128)(2,1)}, bf16[1,2,128,1280]{3,2,1,0:T(8,128)(2,1)}, bf16[1,2,128,1280]{3,2,1,0:T(8,128)(2,1)}), (bf16[1,2,128,1280]{3,2,1,0:T(8,128)(2,1)}, bf16[1,2,128,1280]{3,2,1,0:T(8,128)(2,1)}, ...) | async-done | bytes 1966096 | tf_op jit(solution)/shard_map/psum | solution.py:15
  115.1 0.0 copy-start.7
  115.1 1.2 constant_dynamic-update-slice_fusion.2
  116.3 1.1 constant_dynamic-update-slice_fusion.1
  117.4 0.0 copy-done.7
  117.5 0.3 multiply_reduce_fusion.1
  117.7 1.2 fusion.20
  118.9 0.0 copy-start.8
  118.9 6.9 all-reduce
  125.9 3.4 copy.50
  129.3 3.7 reshape_reshape_squeeze.3
  132.9 0.0 copy-done.8
  132.9 2.7 fusion.10
  135.6 2.4 copy.47
  138.0 2.6 copy.46
  140.7 0.0 copy-start.9
  140.7 3.1 reshape.127
  143.8 0.0 copy-start.2
  143.8 0.0 copy-done.9
  143.8 7.8 fusion.22
  151.6 0.0 copy-done.2
  151.6 3.6 fusion.7
  155.2 0.0 copy-start.1
  155.2 1.9 copy-done.1
  157.1 1.4 convolution_bitcast_fusion
  158.5 1.8 copy.60
  160.4 0.0 copy-start.6
  160.4 4.0 fusion.11
  164.4 0.0 copy-done.6
  164.4 0.0 copy-start.4
  164.4 4.4 fusion.2
  168.7 0.0 copy-start
  168.8 1.9 copy-done
  170.6 0.0 copy-done.4
  170.6 2.1 convolution_bitcast_fusion.1
  172.8 2.7 stack_reshape.6
  175.5 4.0 stack_reshape.7
  179.5 5.0 pad_maximum_fusion
  184.6 6.7 copy.61
  191.2 0.0 copy-start.3
  191.2 0.0 all-gather.3.cloned.1.call-update
  191.2 0.6 copy-done.10
  191.9 0.9 copy-done.3
  192.8 3.2 fusion.12
  196.0 0.6 copy.57
  196.6 1.5 copy.62
  198.1 590.5 %all-gather.3.cloned.1.call-done = f32[24,2,128,1280]{3,2,1,0:T(8,128)} async-done(((f32[3,2,128,1280]{3,2,1,0:T(8,128)}), f32[24,2,128,1280]{3,2,1,0:T(8,128)}) %all-gather.3.cloned.1.call-update) | async-done | bytes 31457296 | tf_op jit(solution)/shard_map/all_gather | solution.py:88
  788.6 13.4 %reduce_sum.68 = f32[3,2,128,1280]{3,2,1,0:T(8,128)} reduce(f32[8,3,2,128,1280]{4,3,2,1,0:T(8,128)} %bitcast.52, f32[]{:T(128)} %constant.38.clone.1), dimensions={0}, to_apply=%region_12.13 | reduce | flops 6881280 | bytes 35389444 | tf_op jit(solution)/shard_map/reduce_sum | solution.py:88
  802.0 3.5 multiply_reduce_fusion
  (9 shorter events, 0.1 us)
Async XLA Ops:
  7.2 107.9 %all-reduce.4.cloned.1.call-start = ((), (), s32[]{:S(2)}) async-start(), calls=%async_computation.1 | async-start | bytes 3932160 | tf_op jit(solution)/shard_map/psum | solution.py:15
  13.1 775.5 %all-gather.3.cloned.1.call-start = ((), (), s32[]{:S(2)}) async-start(), calls=%async_computation | async-start | bytes 35389440 | tf_op jit(solution)/shard_map/all_gather | solution.py:88
  13.1 3.2 copy-start.11
  13.1 3.5 copy-start.5
  115.1 2.3 copy-start.7
  118.9 14.0 %copy-start.8 = (f32[1280]{0:T(1024)S(1)}, f32[1280]{0:T(1024)}, u32[]{:S(2)}) copy-start(f32[1280]{0:T(1024)} %param.8) | copy-start | bytes 15364
  140.7 3.1 copy-start.9
  143.8 7.9 copy-start.2
  155.2 1.9 copy-start.1
  160.4 4.0 copy-start.6
  164.4 6.3 copy-start.4
  168.7 1.9 copy-start
  191.2 0.7 copy-start.10
  191.2 1.6 copy-start.3
Sparse Core Ops, SparseCore 0:
  13.2 101.8 all-reduce.3
  191.4 597.1 all-gather.2
